TPU v7x, 32 devices: a whole 2x2x4 slice. The times are simulated.
32 devices in a mesh: grp: 2 (over x), tile: 16 (over z, y, core).
Axes of the slice: x: 2, y: 2, z: 4, core: 2. Of those that a mesh axis runs over, the one named last changes fastest.
Arguments:
- latents: bfloat16 [384, 16, 8, 256], P(('grp', 'tile')), parts along dimension 0, may hold values from -6 to 6
- frame_counts: int32 [32], P('grp'), parts along dimension 0, may hold values from 1 to 12, 64 in all
- clip_order: int32 [32], P('grp'), parts along dimension 0, may hold values from 0 to 15, each once
- norm_scale: float32 [256], replicated, may hold values from 0.25 to 1.75
- norm_offset: float32 [256], replicated, may hold values from -3 to 3
- conv_weight: bfloat16 [3, 3, 3, 256, 256], replicated, may hold values from -0.078125 to 0.078125
- conv_bias: float32 [256], replicated, may hold values from -3 to 3
- out_scale: float32 [256], replicated, may hold values from 0.25 to 1.75
- out_offset: float32 [256], replicated, may hold values from -3 to 3
Outputs:
- block_out: bfloat16 [2, 1024, 8, 256], P(None, ('grp', 'tile')), parts along dimension 1
- normed: bfloat16 [2, 1024, 8, 256], P(None, ('grp', 'tile')), parts along dimension 1
There are 2 independent parts, one for each index of `grp`. A program takes and returns all parts, laid end to end along the dimension named above; an argument that names none is the same for every part. Nothing has to cross between parts.
Inputs may be any that keep to these rules, and one draw needn't show every extreme that they name: `frame_counts`: they sum to 64; the largest is exactly 12. `clip_order`: A permutation of the clips.
All inputs are finite; a program needn't handle non-finite values.
Results may differ from a plain program's by a relative error of at most 0.0057.
Values may be sent and summed in bfloat16 or wider, within the bound.
No kernel may reach another device: no remote copies, remote signals or barrier semaphores. Data moves between devices by JAX's collectives and lax.ppermute only.
A program may use at most 64 MiB of HBM per device.

v0:
```python
import jax
import jax.numpy as jnp
from jax import lax
from jax.sharding import PartitionSpec as P

GROUPS = 32
MEANF = 4
NRB = 8
eps = 1e-06


def normalize(values, frame_count, scaling, offsets):
    frames = values.shape[0]
    channels = values.shape[-1]
    grouped = values.reshape(frames, -1, GROUPS, channels // GROUPS)
    live_mask = (jnp.arange(frames) < frame_count).astype(jnp.float32)[:, None, None, None]
    members = frame_count.astype(jnp.float32) * grouped.shape[1] * grouped.shape[3]
    group_mean = jnp.sum(grouped * live_mask, axis=(0, 1, 3)) / members
    spread = (
        jnp.sum(grouped * grouped * live_mask, axis=(0, 1, 3)) / members - group_mean * group_mean
    )
    inverse = lax.rsqrt(spread + eps)
    normed = (grouped - group_mean[:, None]) * inverse[:, None] * scaling.reshape(
        GROUPS, -1
    ) + offsets.reshape(GROUPS, -1)
    return jax.nn.silu(normed).reshape(values.shape)


def convolve(stacked, kernel, offsets):
    tile_rows = stacked.shape[1] - 2
    columns = stacked.shape[3]
    channels = stacked.shape[4]
    padded = jnp.pad(stacked, ((0, 0), (0, 0), (0, 0), (1, 1), (0, 0)))
    tap_list = [
        padded[frame_lag, row_tap : row_tap + tile_rows, :, col_tap : col_tap + columns]
        for frame_lag in range(3)
        for row_tap in range(3)
        for col_tap in range(3)
    ]
    unfolded = jnp.concatenate(tap_list, axis=-1)
    result = jnp.dot(
        unfolded.reshape(-1, 27 * channels),
        kernel.reshape(27 * channels, -1),
        preferred_element_type=jnp.float32,
    )
    return (result + offsets).reshape(tile_rows, stacked.shape[2], columns, -1)


def local(
    latents,
    frame_counts,
    clip_order,
    norm_scale,
    norm_offset,
    conv_weight,
    conv_bias,
    out_scale,
    out_offset,
):
    devices = lax.axis_size("tile")
    device = lax.axis_index("tile")
    frames, frame_rows, columns, channels = latents.shape
    tile_rows = frame_rows // NRB
    own_tiles = frames * NRB
    capacity = (own_tiles + devices - 1) // devices
    slots_all = devices * capacity
    worker_tiles = MEANF * NRB
    positions = jnp.arange(frame_counts.shape[0], dtype=jnp.int32)
    chosen = clip_order[:, None] == positions[None, :]
    ordered = jnp.sum(jnp.where(chosen, frame_counts[None, :], 0), axis=1)
    starts = (jnp.cumsum(ordered) - ordered) * NRB
    own_start = jnp.sum(jnp.where(clip_order == device, starts, 0))
    own_count = jnp.sum(jnp.where(positions == device, frame_counts, 0))
    active = normalize(latents.astype(jnp.float32), own_count, norm_scale, norm_offset).astype(
        jnp.bfloat16
    )
    outgoing_slot = jnp.arange(slots_all, dtype=jnp.int32)
    target = outgoing_slot // capacity
    source_tile = outgoing_slot % capacity * devices + (target - own_start) % devices
    sendable = source_tile < own_count * NRB
    source_tile = jnp.minimum(source_tile, own_tiles - 1)
    local_slot = jnp.arange(worker_tiles, dtype=jnp.int32)
    tile_id = local_slot * devices + device
    placed = jnp.sum((starts[None, :] <= tile_id[:, None]).astype(jnp.int32), axis=1) - 1
    at_place = placed[:, None] == positions[None, :]
    clip_id = jnp.sum(jnp.where(at_place, clip_order[None, :], 0), axis=1)
    within = tile_id - jnp.sum(jnp.where(at_place, starts[None, :], 0), axis=1)
    take_from = clip_id * capacity + within // devices
    padded = jnp.pad(active, ((2, 0), (1, 1), (0, 0), (0, 0)))
    lagged = []
    for frame_lag in range(3):
        window = padded[frame_lag : frame_lag + frames]
        row_bands = [
            window[:, row_start : row_start + NRB * tile_rows : tile_rows]
            for row_start in range(tile_rows + 2)
        ]
        lagged.append(jnp.stack(row_bands, 0))
    pieces = jnp.stack(lagged, 0).reshape(3, tile_rows + 2, own_tiles, columns, channels)
    outgoing = jnp.where(
        sendable[None, None, :, None, None], jnp.take(pieces, source_tile, axis=2), 0
    )
    received = lax.all_to_all(outgoing, "tile", split_axis=2, concat_axis=2, tiled=True)
    stacked = jnp.take(received, take_from, axis=2)
    block_out = convolve(stacked, conv_weight, conv_bias).astype(jnp.bfloat16)
    per_group = channels // GROUPS
    grouped = block_out.astype(jnp.float32).reshape(
        tile_rows, worker_tiles, columns, GROUPS, per_group
    )
    first_sum = jnp.sum(grouped, axis=(0, 2, 4))
    second_sum = jnp.sum(grouped * grouped, axis=(0, 2, 4))
    belongs = (clip_id[:, None] == positions[None, :]).astype(jnp.float32)
    totals = lax.psum(
        (
            jnp.dot(belongs.T, first_sum, precision=lax.Precision.HIGHEST),
            jnp.dot(belongs.T, second_sum, precision=lax.Precision.HIGHEST),
        ),
        "tile",
    )
    members = frame_counts.astype(jnp.float32) * (frame_rows * columns * per_group)
    clip_mean = totals[0] / members[:, None]
    clip_spread = totals[1] / members[:, None] - clip_mean * clip_mean
    clip_inverse = lax.rsqrt(clip_spread + eps)
    tile_mean = jnp.dot(belongs, clip_mean, precision=lax.Precision.HIGHEST)
    tile_inverse = jnp.dot(belongs, clip_inverse, precision=lax.Precision.HIGHEST)
    normed = (grouped - tile_mean[None, :, None, :, None]) * tile_inverse[
        None, :, None, :, None
    ] * out_scale.reshape(GROUPS, per_group) + out_offset.reshape(GROUPS, per_group)
    normed = jax.nn.silu(normed).astype(jnp.bfloat16).reshape(block_out.shape)
    return (block_out, normed)


def solution(mesh):
    in_specs = (
        P(("grp", "tile"), None, None, None),
        P("grp"),
        P("grp"),
        P(),
        P(),
        P(),
        P(),
        P(),
        P(),
    )
    out_specs = (P(None, ("grp", "tile"), None, None), P(None, ("grp", "tile"), None, None))
    return jax.shard_map(local, mesh=mesh, in_specs=in_specs, out_specs=out_specs, check_vma=False)
```

profile of v0, /device:TPU:0, one launch (start us, length us, event | category | flops | bytes accessed | tf_op | source)
XLA Modules:
  0.0 250.5 jit_solution(12813425869111469504)
XLA Ops:
  0.6 0.0 copy-start
  0.6 1.0 select_reduce_fusion.2
  1.7 0.0 copy-start.4
  1.7 0.5 copy-done.4
  2.2 0.1 copy.82
  2.3 0.1 reduce.4
  2.4 2.0 fusion.32
  4.4 0.6 compare_convert_fusion
  5.5 1.2 fusion.39
  6.7 1.3 compare_and_fusion
  8.0 2.2 fusion.11
  10.3 0.8 reduce_sum.113
  11.0 1.4 reduce_sum.116
  12.4 0.6 reduce_sum.114
  13.0 0.8 reduce_sum.117
  13.9 1.2 add_rsqrt_fusion
  15.0 0.1 mul.181
  15.1 0.7 mul.182
  15.8 0.7 sub.107
  16.5 0.7 sub.108
  17.1 1.7 fusion.9
  18.9 0.2 pad_slice_fusion.20
  19.1 0.0 copy-start.6
  19.1 1.3 fusion.44
  20.3 1.2 fusion.46
  21.6 1.2 fusion.45
  22.7 0.0 copy-done.6
  23.3 0.7 broadcast_compare_fusion
  24.0 5.2 %maximum_maximum_fusion = bf16[3,4,96,8,256]{4,3,2,1,0:T(8,128)(2,1)} fusion(bf16[1,1,96,8,256]{4,3,2,1,0:T(8,128)(2,1)} %bitcast.72, bf16[1,1,96,8,256]{4,3,2,1,0:T(8,128)(2,1)} %bitcast.73, bf16[1,1,96,8,256]{4,3,2,1,0:T(8,128)(2,1)} %bitcast.74, bf16[1,1,96,8,256]{4,3,2,1,0:T(8,128)(2,1)} %bitcast.71, bf16[1,1,96,8,256]{4,3,2,1,0:T(8,128)(2,1)} %bitcast.76, ...), kind=kLoop, calls=%fused_computation.21 | loop fusion | flops 25952256 | bytes 9437184 | tf_op jit(solution)/shard_map/stack | solution.py:98
  29.2 5.9 %gather_fusion = bf16[96,3,4,8,256]{4,3,2,1,0:T(8,128)(2,1)} fusion(bf16[3,4,96,8,256]{4,3,2,1,0:T(8,128)(2,1)} %maximum_maximum_fusion, s32[1024]{0:T(1024)S(1)} %pad_clamp_fusion.1), kind=kCustom, calls=%fused_computation | custom fusion | bytes 9437568 | tf_op jit(solution)/shard_map/jit(_take)/gather | solution.py:100
  35.1 0.0 copy-done.5
  35.1 5.1 %select_bitcast_fusion = bf16[3,4,96,8,256]{4,3,1,0,2:T(8,128)(2,1)} fusion(bf16[96,3,4,8,256]{4,3,2,1,0:T(8,128)(2,1)} %gather_fusion, pred[96]{0:T(512)(128)(4,1)S(1)} %broadcast_compare_fusion, pred[96]{0:T(512)(128)(4,1)S(1)} %copy-done.5), kind=kLoop, calls=%fused_computation.22 | loop fusion | flops 4718592 | bytes 9437376 | tf_op jit(solution)/shard_map/jit(_where)/select_n | solution.py:99
  40.2 0.0 copy-start.3
  40.2 0.0 copy-start.2
  40.2 7.6 %all-to-all-start = ((bf16[3,4,96,8,256]{4,3,1,0,2:T(8,128)(2,1)}), bf16[3,4,96,8,256]{4,3,1,0,2:T(8,128)(2,1)}, u32[]{:S(2)}, u32[]{:S(2)}) async-start(bf16[3,4,96,8,256]{4,3,1,0,2:T(8,128)(2,1)} %select_bitcast_fusion), calls=%async_computation | async-start | bytes 9437184 | tf_op jit(solution)/shard_map/all_to_all | solution.py:102
  47.8 0.0 copy-done.3
  47.8 0.1 convert_reduce_fusion
  47.9 0.0 copy-done.2
  47.9 0.1 select_reduce_fusion.1
  48.0 0.0 copy-start.1
  48.1 1.2 convert_multiply_fusion.2
  49.3 85.3 %all-to-all-done = bf16[3,4,96,8,256]{4,3,1,0,2:T(8,128)(2,1)} async-done(((bf16[3,4,96,8,256]{4,3,1,0,2:T(8,128)(2,1)}), bf16[3,4,96,8,256]{4,3,1,0,2:T(8,128)(2,1)}, u32[]{:S(2)}, u32[]{:S(2)}) %all-to-all-start) | async-done | bytes 4718624 | tf_op jit(solution)/shard_map/all_to_all | solution.py:102
  134.6 4.9 %copy.83 = bf16[3,4,96,8,256]{4,3,2,1,0:T(8,128)(2,1)} copy(bf16[3,4,96,8,256]{4,3,1,0,2:T(8,128)(2,1)} %all-to-all-done) | data formatting | bytes 9437184 | tf_op jit(solution)/shard_map/all_to_all | solution.py:102
  139.5 4.2 %gather_fusion.1 = bf16[32,3,4,8,256]{4,3,2,1,0:T(8,128)(2,1)} fusion(bf16[3,4,96,8,256]{4,3,2,1,0:T(8,128)(2,1)} %copy.83, s32[1024]{0:T(1024)S(1)} %pad_clamp_fusion), kind=kCustom, calls=%fused_computation.1 | custom fusion | bytes 3145856 | tf_op jit(solution)/shard_map/jit(_take)/gather | solution.py:103
  143.8 1.6 select_bitcast_fusion.1
  145.4 0.2 fusion.43
  145.6 1.2 pad_slice_fusion
  147.8 0.0 copy-start.7
  148.3 0.0 copy-done
  148.3 0.2 copy-done.7
  148.5 2.7 %fusion.12 = bf16[512,256]{1,0:T(8,128)(2,1)} fusion(bf16[512,6912]{1,0:T(8,128)(2,1)S(1)} %constant_dynamic-update-slice_fusion, bf16[6912,256]{1,0:T(8,128)(2,1)S(1)} %bitcast.66, f32[256]{0:T(256)S(1)} %copy-done.7), kind=kOutput, calls=%fused_computation.40 | convolution fusion | flops 1812201472 | bytes 10880000 | tf_op jit(solution)/shard_map/dot_general | solution.py:41
  151.2 7.0 %reshape.406 = f32[2,32,8,32,8]{4,3,2,1,0:T(8,128)} reshape(bf16[512,256]{1,0:T(8,128)(2,1)} %fusion.12) | data formatting | bytes 786432 | tf_op jit(solution)/shard_map/convert_element_type | solution.py:106
  158.2 5.0 %fusion.42 = (f32[32,32]{1,0:T(8,128)S(1)}, f32[32,32]{1,0:T(8,128)S(1)}) fusion(f32[2,32,8,32,8]{4,3,2,1,0:T(8,128)} %reshape.406), kind=kLoop, calls=%fused_computation.154 | loop fusion | flops 391168 | bytes 532480 | tf_op jit(solution)/shard_map/reduce_sum | solution.py:109
  163.2 0.0 copy-done.1
  163.2 0.3 fusion.16
  163.5 0.9 fusion.14
  164.4 77.8 %all-reduce.2 = (f32[16,32]{1,0:T(8,128)}, f32[16,32]{1,0:T(8,128)}) all-reduce(f32[16,32]{1,0:T(8,128)S(1)} %fusion.14, f32[16,32]{1,0:T(8,128)S(1)} %fusion.16), channel_id=1, replica_groups=mesh['grp'=2,'tile'=16] {'tile'}, use_global_device_ids=true, to_apply=%region_14.15 | all-reduce | flops 1024 | bytes 8192 | tf_op jit(solution)/shard_map/psum | solution.py:112
  242.2 1.0 fusion.15
  243.1 0.7 broadcast_bitcast_fusion.1
  243.8 1.6 copy.112
  245.4 1.0 fusion.13
  246.4 0.7 broadcast_bitcast_fusion
  247.1 1.6 copy.114
  248.7 1.9 multiply_convert_fusion
  (62 shorter events, 1.1 us)
Async XLA Ops:
  0.6 147.7 %copy-start = (bf16[3,3,3,256,256]{4,3,2,1,0:T(8,128)(2,1)S(1)}, bf16[3,3,3,256,256]{4,3,2,1,0:T(8,128)(2,1)}, u32[]{:S(2)}) copy-start(bf16[3,3,3,256,256]{4,3,2,1,0:T(8,128)(2,1)} %param.14) | copy-start | bytes 10616836
  1.7 0.5 copy-start.4
  19.1 3.7 %copy-start.6 = (s32[96]{0:T(128)S(1)}, s32[96]{0:T(128)}, u32[]{:S(2)}) copy-start(s32[96]{0:T(128)} %fusion.39) | copy-start | bytes 1156
  29.2 5.9 %copy-start.5 = (pred[96]{0:T(512)(128)(4,1)S(1)}, pred[96]{0:T(512)(128)(4,1)}, u32[]{:S(2)}) copy-start(pred[96]{0:T(512)(128)(4,1)} %compare_and_fusion) | copy-start | bytes 292
  40.2 7.6 %copy-start.3 = (s32[16]{0:T(128)S(1)}, s32[16]{0:T(128)}, u32[]{:S(2)}) copy-start(s32[16]{0:T(128)} %get-tuple-element.11) | copy-start | bytes 196
  40.2 7.7 %copy-start.2 = (s32[16]{0:T(128)S(1)}, s32[16]{0:T(128)}, u32[]{:S(2)}) copy-start(s32[16]{0:T(128)} %param.11) | copy-start | bytes 196
  40.2 94.4 %all-to-all-start = ((bf16[3,4,96,8,256]{4,3,1,0,2:T(8,128)(2,1)}), bf16[3,4,96,8,256]{4,3,1,0,2:T(8,128)(2,1)}, u32[]{:S(2)}, u32[]{:S(2)}) async-start(bf16[3,4,96,8,256]{4,3,1,0,2:T(8,128)(2,1)} %select_bitcast_fusion), calls=%async_computation | async-start | bytes 9437184 | tf_op jit(solution)/shard_map/all_to_all | solution.py:102
  48.0 115.2 %copy-start.1 = (s32[32]{0:T(128)}, s32[32]{0:T(128)S(1)}, u32[]{:S(2)}) copy-start(s32[32]{0:T(128)S(1)} %get-tuple-element.6) | copy-start | bytes 388
  147.8 0.7 copy-start.7
where the time goes:
time: 252 us; the launch traced here: 251 us
  waiting for transfers between devices  85.3 us (34%)
  blocking collectives  77.8 us (31%)
  local copies, waits for them, and re-layouts  37.9 us (15%)
  other arithmetic  33.9 us (13%)
  starting transfers between devices  7.56 us (3%)
  matrix products  5.83 us (2%)
    all_to_all x1, waiting for transfers between devices, local(): lax.all_to_all(outgoing, 'tile', split_axis=2, concat_axis=2, tiled=True)  85.3 us
    psum x1, blocking collectives, local(): lax.psum((jnp.dot(belongs.T, first_sum, precision=lax.Precision.HIGHEST),...  77.8 us
    all_to_all x1, starting transfers between devices, local(): lax.all_to_all(outgoing, 'tile', split_axis=2, concat_axis=2, tiled=True)  7.56 us
    convert_element_type x1, local copies, waits for them, and re-layouts, local(): block_out.astype(jnp.float32)  7 us
    gather x1, local copies, waits for them, and re-layouts, local(): jnp.take(pieces, source_tile, axis=2)  5.85 us
    another operation x1, other arithmetic, local(): jnp.stack(lagged, 0).reshape(3, tile_rows + 2, own_tiles, columns, channels)  5.21 us
    select_n x1, other arithmetic, local(): jnp.where(sendable[None, None, :, None, None], jnp.take(pieces, source_ti...  5.14 us
  transfers between devices with their start and end apart: 1, of which 1 were waited for; matrix products, arithmetic and copies ran while one was open for 1% of the time, Pallas kernels for 0%

commit v1 on v0

--- a/solution.py
+++ b/solution.py
@@ -7,6 +7,17 @@
 MEANF = 4
 NRB = 8
 eps = 1e-06
+
+
+def in_blocks(array, dim, peers):
+    before, after = (array.shape[:dim], array.shape[dim + 1 :])
+    return jnp.moveaxis(array.reshape(*before, peers, -1, *after), dim, 0)
+
+
+def laid_out(blocks, dim):
+    dims = list(blocks.shape[1:])
+    dims[dim] *= blocks.shape[0]
+    return jnp.moveaxis(blocks, 0, dim).reshape(dims)
 
 
 def normalize(values, frame_count, scaling, offsets):
@@ -99,7 +110,14 @@
     outgoing = jnp.where(
         sendable[None, None, :, None, None], jnp.take(pieces, source_tile, axis=2), 0
     )
-    received = lax.all_to_all(outgoing, "tile", split_axis=2, concat_axis=2, tiled=True)
+    peers, index = (lax.axis_size("tile"), lax.axis_index("tile"))
+    pieces_2 = in_blocks(outgoing, 2, peers)
+    gathered = [pieces_2[index]]
+    for turn in range(1, peers):
+        sent = pieces_2[index ^ turn]
+        gathered.append(lax.ppermute(sent, "tile", [(i, i ^ turn) for i in range(peers)]))
+    pieces_2 = jnp.stack(gathered)[index ^ jnp.arange(peers)]
+    received = laid_out(pieces_2, 2)
     stacked = jnp.take(received, take_from, axis=2)
     block_out = convolve(stacked, conv_weight, conv_bias).astype(jnp.bfloat16)
     per_group = channels // GROUPS

time: 252 us -> 264 us (1.048)
  waiting for transfers between devices: 85.3 us -> 36.5 us
  starting transfers between devices: 7.56 us -> 44.2 us
  local copies, waits for them, and re-layouts: 37.9 us -> 67.2 us
    all_to_all x1 -> x0, waiting for transfers between devices: 85.3 us -> none  [local(): lax.all_to_all(outgoing, 'tile', split_axis=2, concat_axis=2, tiled=True)]
    ppermute x0 -> x15, starting transfers between devices: none -> 44.2 us  [local(): lax.ppermute(sent, 'tile', [(i, i ^ turn) for i in range(peers)])]
    ppermute x0 -> x15, waiting for transfers between devices: none -> 36.5 us  [local(): lax.ppermute(sent, 'tile', [(i, i ^ turn) for i in range(peers)])]
    unnamed x42 -> x67, local copies, waits for them, and re-layouts: 1.22 us -> 20.6 us
    all_to_all x1 -> x0, starting transfers between devices: 7.56 us -> none  [local(): lax.all_to_all(outgoing, 'tile', split_axis=2, concat_axis=2, tiled=True)]
    gather x0 -> x1, local copies, waits for them, and re-layouts: none -> 5.31 us  [local(): pieces_2 = jnp.stack(gathered)[index ^ jnp.arange(peers)]]
    transpose x0 -> x1, local copies, waits for them, and re-layouts: none -> 5.02 us  [laid_out(): return jnp.moveaxis(blocks, 0, dim).reshape(dims)]
    all_to_all x1 -> x0, local copies, waits for them, and re-layouts: 4.91 us -> none  [local(): lax.all_to_all(outgoing, 'tile', split_axis=2, concat_axis=2, tiled=True)]
  transfers between devices with their start and end apart: 1 -> 15, of which waited for: 1 -> 5; matrix products, arithmetic and copies ran while one was open for 1% -> 8% of each run, Pallas kernels for 0% -> 0%
where the time goes in v1:
time: 264 us; the launch traced here: 263 us
  blocking collectives  75.2 us (28%)
  local copies, waits for them, and re-layouts  67.2 us (25%)
  starting transfers between devices  44.2 us (17%)
  waiting for transfers between devices  36.5 us (14%)
  other arithmetic  31.6 us (12%)
  matrix products  5.76 us (2%)
  between operations  2.66 us (1%)
    psum x1, blocking collectives, local(): lax.psum((jnp.dot(belongs.T, first_sum, precision=lax.Precision.HIGHEST),...  75.2 us
    ppermute x15, starting transfers between devices, local(): lax.ppermute(sent, 'tile', [(i, i ^ turn) for i in range(peers)])  44.2 us
    ppermute x15, waiting for transfers between devices, local(): lax.ppermute(sent, 'tile', [(i, i ^ turn) for i in range(peers)])  36.5 us
    unnamed x67, local copies, waits for them, and re-layouts  20.6 us
    gather x2, local copies, waits for them, and re-layouts, local(): jnp.take(pieces, source_tile, axis=2)  10.7 us
    convert_element_type x1, local copies, waits for them, and re-layouts, local(): block_out.astype(jnp.float32)  7 us
    gather x1, local copies, waits for them, and re-layouts, local(): pieces_2 = jnp.stack(gathered)[index ^ jnp.arange(peers)]  5.31 us
  transfers between devices with their start and end apart: 15, of which 5 were waited for; matrix products, arithmetic and copies ran while one was open for 8% of the time, Pallas kernels for 0%

profile of v1, /device:TPU:0, one launch (start us, length us, event | category | flops | bytes accessed | tf_op | source)
XLA Modules:
  0.0 263.1 jit_solution(8258598755422816899)
XLA Ops:
  0.6 1.0 select_reduce_fusion.2
  2.4 1.9 fusion.38
  5.6 1.2 fusion.44
  6.8 1.2 compare_and_fusion
  8.7 2.3 fusion.11
  11.0 0.8 reduce_sum.113
  11.7 1.4 reduce_sum.116
  13.1 0.7 reduce_sum.114
  13.8 0.8 reduce_sum.117
  14.6 1.3 add_rsqrt_fusion
  16.6 0.7 sub.108
  17.3 0.7 sub.109
  18.0 1.7 fusion.9
  20.6 3.4 %maximum_maximum_fusion = bf16[3,4,96,8,256]{4,3,2,1,0:T(8,128)(2,1)} fusion(bf16[1,1,96,8,256]{4,3,2,1,0:T(8,128)(2,1)S(1)} %bitcast.142, bf16[1,1,96,8,256]{4,3,2,1,0:T(8,128)(2,1)S(1)} %bitcast.143, bf16[1,1,96,8,256]{4,3,2,1,0:T(8,128)(2,1)S(1)} %bitcast.144, bf16[1,1,96,8,256]{4,3,2,1,0:T(8,128)(2,1)S(1)} %bitcast.141, ...), kind=kLoop, calls=%fused_computation.22 | loop fusion | flops 25952256 | bytes 9437184 | tf_op jit(solution)/shard_map/stack | solution.py:109
  24.0 5.8 %gather_fusion = bf16[96,3,4,8,256]{4,3,2,1,0:T(8,128)(2,1)} fusion(bf16[3,4,96,8,256]{4,3,2,1,0:T(8,128)(2,1)} %maximum_maximum_fusion, s32[1024]{0:T(1024)S(1)} %pad_clamp_fusion.2), kind=kCustom, calls=%fused_computation | custom fusion | bytes 9437568 | tf_op jit(solution)/shard_map/jit(_take)/gather | solution.py:111
  29.8 4.9 %copy.149 = bf16[3,4,96,8,256]{4,3,2,1,0:T(8,128)(2,1)} copy(bf16[3,4,96,8,256]{4,3,1,0,2:T(8,128)(2,1)} %bitcast.134) | data formatting | bytes 9437184 | tf_op jit(solution)/shard_map/jit(_take)/gather | solution.py:111
  35.5 3.1 %select_select_fusion = bf16[3,4,16,6,8,256]{5,4,3,2,1,0:T(8,128)(2,1)S(1)} fusion(bf16[3,4,16,6,8,256]{5,4,3,2,1,0:T(8,128)(2,1)} %bitcast.133, pred[16,6]{1,0:T(8,128)(4,1)S(1)} %copy-done.5, pred[16,6]{1,0:T(8,128)(4,1)S(1)} %broadcast_compare_fusion), kind=kLoop, calls=%fused_computation.23 | loop fusion | flops 4718592 | bytes 9437376 | tf_op jit(solution)/shard_map/jit(_where)/select_n | solution.py:110
  38.6 2.1 copy-done.1
  40.7 2.2 dynamic-slice_bitcast_fusion
  43.3 2.5 collective-permute-start.1
  46.0 1.8 collective-permute-start.3
  49.0 1.8 bitcast_dynamic-update-slice_fusion.15
  51.4 1.2 convert_multiply_fusion.2
  52.7 2.6 %collective-permute-start.5 = (bf16[3,4,6,8,256]{4,3,2,1,0:T(8,128)(2,1)}, bf16[3,4,6,8,256]{4,3,2,1,0:T(8,128)(2,1)S(1)}, u32[]{:S(2)}, u32[]{:S(2)}) collective-permute-start(bf16[3,4,6,8,256]{4,3,2,1,0:T(8,128)(2,1)} %get-tuple-element.23), channel_id=1, source_target_pairs={{0,6},{1,7},{2,4},{3,5},{4,2},{5,3},{6,0},{7,1},{8,14},{9,15},{10,... | collective-permute-start | bytes 884744 | tf_op jit(solution)/shard_map/ppermute | solution.py:118
  55.3 1.7 bitcast_dynamic-update-slice_fusion.14
  57.1 1.7 bitcast_dynamic-update-slice_fusion.13
  58.8 1.1 collective-permute-done.2
  59.9 2.6 collective-permute-start.7
  62.6 1.7 bitcast_dynamic-update-slice_fusion.12
  64.4 1.7 bitcast_dynamic-update-slice_fusion.11
  66.1 3.6 %collective-permute-start.9 = (bf16[3,4,6,8,256]{4,3,2,1,0:T(8,128)(2,1)}, bf16[3,4,6,8,256]{4,3,2,1,0:T(8,128)(2,1)S(1)}, u32[]{:S(2)}, u32[]{:S(2)}) collective-permute-start(bf16[3,4,6,8,256]{4,3,2,1,0:T(8,128)(2,1)} %get-tuple-element.19), channel_id=1, source_target_pairs={{0,10},{1,11},{2,8},{3,9},{4,14},{5,15},{6,12},{7,13},{8,2},{9,3},... | collective-permute-start | bytes 884744 | tf_op jit(solution)/shard_map/ppermute | solution.py:118
  69.7 1.7 bitcast_dynamic-update-slice_fusion.10
  71.3 10.9 %collective-permute-done.5 = bf16[3,4,6,8,256]{4,3,2,1,0:T(8,128)(2,1)S(1)} collective-permute-done((bf16[3,4,6,8,256]{4,3,2,1,0:T(8,128)(2,1)}, bf16[3,4,6,8,256]{4,3,2,1,0:T(8,128)(2,1)S(1)}, u32[]{:S(2)}, u32[]{:S(2)}) %collective-permute-start.5) | collective-permute-done | bytes 294944 | tf_op jit(solution)/shard_map/ppermute | solution.py:118
  82.2 0.7 bitcast_dynamic-update-slice_fusion.9
  83.0 4.3 %collective-permute-done.6 = bf16[3,4,6,8,256]{4,3,2,1,0:T(8,128)(2,1)S(1)} collective-permute-done((bf16[3,4,6,8,256]{4,3,2,1,0:T(8,128)(2,1)}, bf16[3,4,6,8,256]{4,3,2,1,0:T(8,128)(2,1)S(1)}, u32[]{:S(2)}, u32[]{:S(2)}) %collective-permute-start.6) | collective-permute-done | bytes 294944 | tf_op jit(solution)/shard_map/ppermute | solution.py:118
  87.2 1.4 collective-permute-start.11
  88.6 0.7 bitcast_dynamic-update-slice_fusion.8
  89.4 2.3 collective-permute-start.12
  91.6 0.8 bitcast_dynamic-update-slice_fusion.7
  92.4 26.6 %collective-permute-start.13 = (bf16[3,4,6,8,256]{4,3,2,1,0:T(8,128)(2,1)S(1)}, bf16[3,4,6,8,256]{4,3,2,1,0:T(8,128)(2,1)S(1)}, u32[]{:S(2)}, u32[]{:S(2)}) collective-permute-start(bf16[3,4,6,8,256]{4,3,2,1,0:T(8,128)(2,1)S(1)} %copy-done.3), channel_id=1, source_target_pairs={{0,14},{1,15},{2,12},{3,13},{4,10},{5,11},{6,8},{7,9},{8,6},{9,7},... | collective-permute-start | bytes 884744 | tf_op jit(solution)/shard_map/ppermute | solution.py:118
  119.0 0.7 bitcast_dynamic-update-slice_fusion.6
  119.7 9.1 %collective-permute-done.9 = bf16[3,4,6,8,256]{4,3,2,1,0:T(8,128)(2,1)S(1)} collective-permute-done((bf16[3,4,6,8,256]{4,3,2,1,0:T(8,128)(2,1)}, bf16[3,4,6,8,256]{4,3,2,1,0:T(8,128)(2,1)S(1)}, u32[]{:S(2)}, u32[]{:S(2)}) %collective-permute-start.9) | collective-permute-done | bytes 294944 | tf_op jit(solution)/shard_map/ppermute | solution.py:118
  128.8 0.7 bitcast_dynamic-update-slice_fusion.5
  129.5 11.1 %collective-permute-done.10 = bf16[3,4,6,8,256]{4,3,2,1,0:T(8,128)(2,1)S(1)} collective-permute-done((bf16[3,4,6,8,256]{4,3,2,1,0:T(8,128)(2,1)}, bf16[3,4,6,8,256]{4,3,2,1,0:T(8,128)(2,1)S(1)}, u32[]{:S(2)}, u32[]{:S(2)}) %collective-permute-start.10) | collective-permute-done | bytes 294944 | tf_op jit(solution)/shard_map/ppermute | solution.py:118
  140.6 0.7 bitcast_dynamic-update-slice_fusion.4
  141.4 0.8 bitcast_dynamic-update-slice_fusion.3
  142.2 0.8 bitcast_dynamic-update-slice_fusion.2
  142.9 0.8 bitcast_dynamic-update-slice_fusion.1
  143.7 0.8 bitcast_dynamic-update-slice_fusion
  144.5 5.3 %gather_fusion.1 = bf16[16,3,4,6,8,256]{5,4,3,2,1,0:T(8,128)(2,1)} fusion(bf16[16,3,4,6,8,256]{5,4,3,2,1,0:T(8,128)(2,1)} %bitcast_dynamic-update-slice_fusion, s32[1024]{0:T(1024)S(1)} %pad_clamp_fusion.1), kind=kCustom, calls=%fused_computation.1 | custom fusion | bytes 9437248 | tf_op jit(solution)/shard_map/gather | solution.py:119
  149.8 5.0 %copy.150 = bf16[3,4,16,6,8,256]{5,4,3,2,1,0:T(8,128)(2,1)} copy(bf16[3,4,16,6,8,256]{5,4,3,1,0,2:T(8,128)(2,1)} %bitcast.135) | data formatting | bytes 9437184 | tf_op jit(solution)/shard_map/transpose | solution.py:20
  154.8 4.2 %gather_fusion.2 = bf16[32,3,4,8,256]{4,3,2,1,0:T(8,128)(2,1)} fusion(bf16[3,4,96,8,256]{4,3,2,1,0:T(8,128)(2,1)} %bitcast.136, s32[1024]{0:T(1024)S(1)} %pad_clamp_fusion), kind=kCustom, calls=%fused_computation.2 | custom fusion | bytes 3145856 | tf_op jit(solution)/shard_map/jit(_take)/gather | solution.py:121
  159.0 1.6 select_bitcast_fusion
  160.9 1.2 pad_slice_fusion
  163.7 2.7 %fusion.12 = bf16[512,256]{1,0:T(8,128)(2,1)} fusion(bf16[512,6912]{1,0:T(8,128)(2,1)S(1)} %constant_dynamic-update-slice_fusion, bf16[6912,256]{1,0:T(8,128)(2,1)S(1)} %bitcast.132, f32[256]{0:T(256)S(1)} %copy-done.12), kind=kOutput, calls=%fused_computation.41 | convolution fusion | flops 1812201472 | bytes 10880000 | tf_op jit(solution)/shard_map/dot_general | solution.py:52
  166.4 7.0 %reshape.467 = f32[2,32,8,32,8]{4,3,2,1,0:T(8,128)} reshape(bf16[512,256]{1,0:T(8,128)(2,1)} %fusion.12) | data formatting | bytes 786432 | tf_op jit(solution)/shard_map/convert_element_type | solution.py:124
  173.4 5.0 %fusion.48 = (f32[32,32]{1,0:T(8,128)S(1)}, f32[32,32]{1,0:T(8,128)S(1)}) fusion(f32[2,32,8,32,8]{4,3,2,1,0:T(8,128)} %reshape.467), kind=kLoop, calls=%fused_computation.194 | loop fusion | flops 391168 | bytes 532480 | tf_op jit(solution)/shard_map/reduce_sum | solution.py:127
  178.7 0.8 fusion.14
  179.6 75.2 %all-reduce.2 = (f32[16,32]{1,0:T(8,128)}, f32[16,32]{1,0:T(8,128)}) all-reduce(f32[16,32]{1,0:T(8,128)S(1)} %fusion.14, f32[16,32]{1,0:T(8,128)S(1)} %fusion.16), channel_id=1, replica_groups=mesh['grp'=2,'tile'=16] {'tile'}, use_global_device_ids=true, to_apply=%region_14.15 | all-reduce | flops 1024 | bytes 8192 | tf_op jit(solution)/shard_map/psum | solution.py:130
  254.8 1.0 fusion.15
  256.4 1.6 copy.179
  258.0 1.0 fusion.13
  259.7 1.6 copy.181
  261.2 1.9 multiply_convert_fusion
  (121 shorter events, 9.5 us)
Async XLA Ops:
  0.6 162.9 %copy-start = (bf16[3,3,3,256,256]{4,3,2,1,0:T(8,128)(2,1)S(1)}, bf16[3,3,3,256,256]{4,3,2,1,0:T(8,128)(2,1)}, u32[]{:S(2)}) copy-start(bf16[3,3,3,256,256]{4,3,2,1,0:T(8,128)(2,1)} %param.14) | copy-start | bytes 10616836
  1.7 0.5 copy-start.9
  19.9 0.7 copy-start.11
  29.8 5.7 %copy-start.5 = (pred[16,6]{1,0:T(8,128)(4,1)S(1)}, pred[16,6]{1,0:T(8,128)(4,1)}, u32[]{:S(2)}) copy-start(pred[16,6]{1,0:T(8,128)(4,1)} %compare_and_fusion) | copy-start | bytes 292
  38.6 2.1 copy-start.1
  40.7 7.6 %copy-start.8 = (s32[16]{0:T(128)S(1)}, s32[16]{0:T(128)}, u32[]{:S(2)}) copy-start(s32[16]{0:T(128)} %get-tuple-element.11) | copy-start | bytes 196
  40.7 7.7 %copy-start.7 = (s32[16]{0:T(128)S(1)}, s32[16]{0:T(128)}, u32[]{:S(2)}) copy-start(s32[16]{0:T(128)} %param.11) | copy-start | bytes 196
  42.9 9.8 %collective-permute-start = (bf16[3,4,6,8,256]{4,3,2,1,0:T(8,128)(2,1)}, bf16[3,4,6,8,256]{4,3,2,1,0:T(8,128)(2,1)}, u32[]{:S(2)}, u32[]{:S(2)}) collective-permute-start(bf16[3,4,6,8,256]{4,3,2,1,0:T(8,128)(2,1)} %get-tuple-element.28), channel_id=1, source_target_pairs={{0,1},{1,0},{2,3},{3,2},{4,5},{5,4},{6,7},{7,6},{8,9},{9,8},{10,11... | collective-permute-start | bytes 884744 | tf_op jit(solution)/shard_map/ppermute | solution.py:118
  43.3 13.7 %collective-permute-start.1 = (bf16[3,4,6,8,256]{4,3,2,1,0:T(8,128)(2,1)}, bf16[3,4,6,8,256]{4,3,2,1,0:T(8,128)(2,1)}, u32[]{:S(2)}, u32[]{:S(2)}) collective-permute-start(bf16[3,4,6,8,256]{4,3,2,1,0:T(8,128)(2,1)} %get-tuple-element.27), channel_id=1, source_target_pairs={{0,2},{1,3},{2,0},{3,1},{4,6},{5,7},{6,4},{7,5},{8,10},{9,11},{10,... | collective-permute-start | bytes 884744 | tf_op jit(solution)/shard_map/ppermute | solution.py:118
  45.8 14.1 %collective-permute-start.2 = (bf16[3,4,6,8,256]{4,3,2,1,0:T(8,128)(2,1)}, bf16[3,4,6,8,256]{4,3,2,1,0:T(8,128)(2,1)}, u32[]{:S(2)}, u32[]{:S(2)}) collective-permute-start(bf16[3,4,6,8,256]{4,3,2,1,0:T(8,128)(2,1)} %get-tuple-element.26), channel_id=1, source_target_pairs={{0,3},{1,2},{2,1},{3,0},{4,7},{5,6},{6,5},{7,4},{8,11},{9,10},{10,... | collective-permute-start | bytes 884744 | tf_op jit(solution)/shard_map/ppermute | solution.py:118
  46.0 18.3 %collective-permute-start.3 = (bf16[3,4,6,8,256]{4,3,2,1,0:T(8,128)(2,1)}, bf16[3,4,6,8,256]{4,3,2,1,0:T(8,128)(2,1)}, u32[]{:S(2)}, u32[]{:S(2)}) collective-permute-start(bf16[3,4,6,8,256]{4,3,2,1,0:T(8,128)(2,1)} %get-tuple-element.25), channel_id=1, source_target_pairs={{0,4},{1,5},{2,6},{3,7},{4,0},{5,1},{6,2},{7,3},{8,12},{9,13},{10,... | collective-permute-start | bytes 884744 | tf_op jit(solution)/shard_map/ppermute | solution.py:118
  47.7 18.3 %collective-permute-start.4 = (bf16[3,4,6,8,256]{4,3,2,1,0:T(8,128)(2,1)}, bf16[3,4,6,8,256]{4,3,2,1,0:T(8,128)(2,1)}, u32[]{:S(2)}, u32[]{:S(2)}) collective-permute-start(bf16[3,4,6,8,256]{4,3,2,1,0:T(8,128)(2,1)} %get-tuple-element.24), channel_id=1, source_target_pairs={{0,5},{1,4},{2,7},{3,6},{4,1},{5,0},{6,3},{7,2},{8,13},{9,12},{10,... | collective-permute-start | bytes 884744 | tf_op jit(solution)/shard_map/ppermute | solution.py:118
  48.5 130.0 %copy-start.6 = (s32[32]{0:T(128)}, s32[32]{0:T(128)S(1)}, u32[]{:S(2)}) copy-start(s32[32]{0:T(128)S(1)} %get-tuple-element.6) | copy-start | bytes 388
  49.0 40.4 %copy-start.4 = (bf16[3,4,6,8,256]{4,3,2,1,0:T(8,128)(2,1)S(1)}, bf16[3,4,6,8,256]{4,3,2,1,0:T(8,128)(2,1)}, u32[]{:S(2)}) copy-start(bf16[3,4,6,8,256]{4,3,2,1,0:T(8,128)(2,1)} %get-tuple-element.16) | copy-start | bytes 884740
  49.0 43.4 %copy-start.3 = (bf16[3,4,6,8,256]{4,3,2,1,0:T(8,128)(2,1)S(1)}, bf16[3,4,6,8,256]{4,3,2,1,0:T(8,128)(2,1)}, u32[]{:S(2)}) copy-start(bf16[3,4,6,8,256]{4,3,2,1,0:T(8,128)(2,1)} %get-tuple-element.15) | copy-start | bytes 884740
  49.0 79.8 %copy-start.2 = (bf16[3,4,6,8,256]{4,3,2,1,0:T(8,128)(2,1)S(1)}, bf16[3,4,6,8,256]{4,3,2,1,0:T(8,128)(2,1)}, u32[]{:S(2)}) copy-start(bf16[3,4,6,8,256]{4,3,2,1,0:T(8,128)(2,1)} %get-tuple-element.14) | copy-start | bytes 884740
  52.7 29.6 %collective-permute-start.5 = (bf16[3,4,6,8,256]{4,3,2,1,0:T(8,128)(2,1)}, bf16[3,4,6,8,256]{4,3,2,1,0:T(8,128)(2,1)S(1)}, u32[]{:S(2)}, u32[]{:S(2)}) collective-permute-start(bf16[3,4,6,8,256]{4,3,2,1,0:T(8,128)(2,1)} %get-tuple-element.23), channel_id=1, source_target_pairs={{0,6},{1,7},{2,4},{3,5},{4,2},{5,3},{6,0},{7,1},{8,14},{9,15},{10,... | collective-permute-start | bytes 884744 | tf_op jit(solution)/shard_map/ppermute | solution.py:118
  57.0 30.2 %collective-permute-start.6 = (bf16[3,4,6,8,256]{4,3,2,1,0:T(8,128)(2,1)}, bf16[3,4,6,8,256]{4,3,2,1,0:T(8,128)(2,1)S(1)}, u32[]{:S(2)}, u32[]{:S(2)}) collective-permute-start(bf16[3,4,6,8,256]{4,3,2,1,0:T(8,128)(2,1)} %get-tuple-element.22), channel_id=1, source_target_pairs={{0,7},{1,6},{2,5},{3,4},{4,3},{5,2},{6,1},{7,0},{8,15},{9,14},{10,... | collective-permute-start | bytes 884744 | tf_op jit(solution)/shard_map/ppermute | solution.py:118
  59.9 29.4 %collective-permute-start.7 = (bf16[3,4,6,8,256]{4,3,2,1,0:T(8,128)(2,1)}, bf16[3,4,6,8,256]{4,3,2,1,0:T(8,128)(2,1)S(1)}, u32[]{:S(2)}, u32[]{:S(2)}) collective-permute-start(bf16[3,4,6,8,256]{4,3,2,1,0:T(8,128)(2,1)} %get-tuple-element.21), channel_id=1, source_target_pairs={{0,8},{1,9},{2,10},{3,11},{4,12},{5,13},{6,14},{7,15},{8,0},{9,1},... | collective-permute-start | bytes 884744 | tf_op jit(solution)/shard_map/ppermute | solution.py:118
  64.3 28.1 %collective-permute-start.8 = (bf16[3,4,6,8,256]{4,3,2,1,0:T(8,128)(2,1)}, bf16[3,4,6,8,256]{4,3,2,1,0:T(8,128)(2,1)S(1)}, u32[]{:S(2)}, u32[]{:S(2)}) collective-permute-start(bf16[3,4,6,8,256]{4,3,2,1,0:T(8,128)(2,1)} %get-tuple-element.20), channel_id=1, source_target_pairs={{0,9},{1,8},{2,11},{3,10},{4,13},{5,12},{6,15},{7,14},{8,1},{9,0},... | collective-permute-start | bytes 884744 | tf_op jit(solution)/shard_map/ppermute | solution.py:118
  66.1 62.7 %collective-permute-start.9 = (bf16[3,4,6,8,256]{4,3,2,1,0:T(8,128)(2,1)}, bf16[3,4,6,8,256]{4,3,2,1,0:T(8,128)(2,1)S(1)}, u32[]{:S(2)}, u32[]{:S(2)}) collective-permute-start(bf16[3,4,6,8,256]{4,3,2,1,0:T(8,128)(2,1)} %get-tuple-element.19), channel_id=1, source_target_pairs={{0,10},{1,11},{2,8},{3,9},{4,14},{5,15},{6,12},{7,13},{8,2},{9,3},... | collective-permute-start | bytes 884744 | tf_op jit(solution)/shard_map/ppermute | solution.py:118
  82.2 58.4 %collective-permute-start.10 = (bf16[3,4,6,8,256]{4,3,2,1,0:T(8,128)(2,1)}, bf16[3,4,6,8,256]{4,3,2,1,0:T(8,128)(2,1)S(1)}, u32[]{:S(2)}, u32[]{:S(2)}) collective-permute-start(bf16[3,4,6,8,256]{4,3,2,1,0:T(8,128)(2,1)} %get-tuple-element.18), channel_id=1, source_target_pairs={{0,11},{1,10},{2,9},{3,8},{4,15},{5,14},{6,13},{7,12},{8,3},{9,2},... | collective-permute-start | bytes 884744 | tf_op jit(solution)/shard_map/ppermute | solution.py:118
  87.2 54.1 %collective-permute-start.11 = (bf16[3,4,6,8,256]{4,3,2,1,0:T(8,128)(2,1)}, bf16[3,4,6,8,256]{4,3,2,1,0:T(8,128)(2,1)S(1)}, u32[]{:S(2)}, u32[]{:S(2)}) collective-permute-start(bf16[3,4,6,8,256]{4,3,2,1,0:T(8,128)(2,1)} %get-tuple-element.17), channel_id=1, source_target_pairs={{0,12},{1,13},{2,14},{3,15},{4,8},{5,9},{6,10},{7,11},{8,4},{9,5},... | collective-permute-start | bytes 884744 | tf_op jit(solution)/shard_map/ppermute | solution.py:118
  89.4 52.8 %collective-permute-start.12 = (bf16[3,4,6,8,256]{4,3,2,1,0:T(8,128)(2,1)S(1)}, bf16[3,4,6,8,256]{4,3,2,1,0:T(8,128)(2,1)S(1)}, u32[]{:S(2)}, u32[]{:S(2)}) collective-permute-start(bf16[3,4,6,8,256]{4,3,2,1,0:T(8,128)(2,1)S(1)} %copy-done.4), channel_id=1, source_target_pairs={{0,13},{1,12},{2,15},{3,14},{4,9},{5,8},{6,11},{7,10},{8,5},{9,4},... | collective-permute-start | bytes 884744 | tf_op jit(solution)/shard_map/ppermute | solution.py:118
  92.4 50.5 %collective-permute-start.13 = (bf16[3,4,6,8,256]{4,3,2,1,0:T(8,128)(2,1)S(1)}, bf16[3,4,6,8,256]{4,3,2,1,0:T(8,128)(2,1)S(1)}, u32[]{:S(2)}, u32[]{:S(2)}) collective-permute-start(bf16[3,4,6,8,256]{4,3,2,1,0:T(8,128)(2,1)S(1)} %copy-done.3), channel_id=1, source_target_pairs={{0,14},{1,15},{2,12},{3,13},{4,10},{5,11},{6,8},{7,9},{8,6},{9,7},... | collective-permute-start | bytes 884744 | tf_op jit(solution)/shard_map/ppermute | solution.py:118
  128.8 14.9 %collective-permute-start.14 = (bf16[3,4,6,8,256]{4,3,2,1,0:T(8,128)(2,1)S(1)}, bf16[3,4,6,8,256]{4,3,2,1,0:T(8,128)(2,1)S(1)}, u32[]{:S(2)}, u32[]{:S(2)}) collective-permute-start(bf16[3,4,6,8,256]{4,3,2,1,0:T(8,128)(2,1)S(1)} %copy-done.2), channel_id=1, source_target_pairs={{0,15},{1,14},{2,13},{3,12},{4,11},{5,10},{6,9},{7,8},{8,7},{9,6},... | collective-permute-start | bytes 884744 | tf_op jit(solution)/shard_map/ppermute | solution.py:118
  149.8 9.3 %copy-start.10 = (pred[32]{0:T(512)(128)(4,1)S(1)}, pred[32]{0:T(512)(128)(4,1)}, u32[]{:S(2)}) copy-start(pred[32]{0:T(512)(128)(4,1)} %compare_and_fusion.1) | copy-start | bytes 100
  163.0 0.7 copy-start.12
